TPU v7x, 512 devices: a whole 4x4x16 slice. The times are simulated.
512 devices in a mesh: space: 32 (over x, y, z_hi), tm: 16 (over z_lo, core).
Axes of the slice: x: 4, y: 4, z: 16 (z_hi: 2, z_lo: 8; z = z_hi * 8 + z_lo), core: 2. Of those that a mesh axis runs over, the one named last changes fastest.
Arguments:
- lattice_field: float32 [64, 128, 2048], P('tm', 'space'), may hold values from -6 to 6
- parity: int32 [16, 32, 128], P('tm', 'space'), may hold values from 0 to 1
- block_list: int32 [16, 8], replicated, may hold values from 0 to 15, as said below
- w_embed: bfloat16 [256, 768], replicated, may hold values from -0.5 to 0.5
- b_embed: float32 [768], replicated, may hold values from -3 to 3
- gain_in: float32 [768], replicated, may hold values from 0.5 to 1.5
- w_qkv: bfloat16 [768, 2304], replicated, may hold values from -4 to 4
- gain_out: float32 [768], replicated, may hold values from 0.5 to 1.5
- w_head: bfloat16 [768, 512], replicated, may hold values from -0.21875 to 0.21875
- b_head: float32 [512], replicated, may hold values from -3 to 3
Outputs:
- new_field: float32 [64, 128, 2048], P('tm', 'space')
- action_density: float32 [64, 128, 2048], P('tm', 'space')
- time_link: float32 [64, 128, 2048], P('tm', 'space')
- slab_link: float32 [64, 128, 2048], P('tm', 'space')
- totals: float32 [2], replicated
Inputs may be any that keep to these rules, and one draw needn't show every extreme that they name: `block_list`: row b lists 8 different block numbers, b among them.
All inputs are finite; a program needn't handle non-finite values.
Results may differ from a plain program's by a relative error of at most 0.006.
Values may be sent and summed in bfloat16 or wider, within the bound.
No kernel may reach another device: no remote copies, remote signals or barrier semaphores. Data moves between devices by JAX's collectives and lax.ppermute only.
A program may use at most 64 MiB of HBM per device.

v0:
```python
import math
import jax
import jax.numpy as jnp
from jax import lax
from jax.sharding import PartitionSpec as P

P_SIZE = 4
D = 768
HEADS = 12
HS = 64
LY = 32
LZ = 64
BLK = 128
hopping = 0.2
quartic = 0.5
epsilon = 1e-05
log_two_pi = math.log(2.0 * math.pi)
floor_score = -1e30


def shifted(x, axis, by):
    length = lax.axis_size(axis)
    return lax.ppermute(x, axis, [(i, (i + by) % length) for i in range(length)])


def layer_norm(values, gain_vec):
    centre = values - jnp.mean(values, axis=-1, keepdims=True)
    spread = jnp.mean(centre * centre, axis=-1, keepdims=True)
    return centre * lax.rsqrt(spread + epsilon) * gain_vec


def site_parity(patch_side):
    positions = jnp.arange(patch_side**4, dtype=jnp.int32)
    return (
        positions // patch_side**3
        + positions // patch_side**2 % patch_side
        + positions // patch_side % patch_side
        + positions % patch_side
    ) % 2


def embed_rows(frozen_in, w_embed, b_embed, gain_in):
    embedded = jnp.dot(frozen_in, w_embed, preferred_element_type=jnp.float32) + b_embed
    return (embedded, layer_norm(embedded, gain_in).astype(jnp.bfloat16))


def attend(carry_in, queries, key_part, value_part, first_key, block_rows):
    running_max, running_sum, running_out = carry_in
    key_rows = key_part.shape[0]
    key_block = (first_key + jnp.arange(key_rows, dtype=jnp.int32)) // BLK
    listed = jnp.any(block_rows[:, :, None] == key_block[None, None, :], axis=1)
    allowed = jnp.repeat(listed, BLK, axis=0)[None]
    query_heads = queries.reshape(queries.shape[0], HEADS, HS)
    scores = jnp.einsum(
        "qhd,khd->hqk",
        query_heads,
        key_part.reshape(key_rows, HEADS, HS),
        preferred_element_type=jnp.float32,
    ) * HS ** (-0.5)
    masked = jnp.where(allowed, scores, floor_score)
    new_max = jnp.maximum(running_max, jnp.max(masked, axis=2))
    exp_scores = jnp.where(allowed, jnp.exp(scores - new_max[:, :, None]), 0.0)
    factor = jnp.exp(running_max - new_max)
    running_sum = running_sum * factor + jnp.sum(exp_scores, axis=2)
    product = jnp.einsum(
        "hqk,khd->hqd",
        exp_scores.astype(jnp.bfloat16),
        value_part.reshape(key_rows, HEADS, HS),
        preferred_element_type=jnp.float32,
    )
    running_out = running_out * factor[:, :, None] + product
    return (new_max, running_sum, running_out)


def fold_rows(carry_in, pieces_in, make_pair, queries, block_rows):
    row_total = pieces_in[0].shape[0]
    pieces_split = tuple(
        (
            piece_arr.reshape((row_total // BLK, BLK) + piece_arr.shape[1:])
            for piece_arr in pieces_in
        )
    )

    def visit_block(carry_now, item_pair):
        position, block_parts = item_pair
        first_key = position * BLK
        block_id = first_key // BLK
        needed = jnp.any(block_rows == block_id)

        def compute_block(carry_here):
            key_part, value_part = make_pair(block_parts)
            return attend(carry_here, queries, key_part, value_part, first_key, block_rows)

        def skip_block(carry_here):
            return carry_here

        return (lax.cond(needed, compute_block, skip_block, carry_now), None)

    carry_out, _ = lax.scan(
        visit_block, carry_in, (jnp.arange(row_total // BLK, dtype=jnp.int32), pieces_split)
    )
    return carry_out


def shards(
    lattice_field, parity, block_list, w_embed, b_embed, gain_in, w_qkv, gain_out, w_head, b_head
):
    tokens_dev = LY // P_SIZE * (LZ // P_SIZE)
    patch_len = P_SIZE**4
    lattice_grid = lattice_field.reshape(
        P_SIZE, P_SIZE, LY // P_SIZE, P_SIZE, LZ // P_SIZE, P_SIZE
    ).transpose(2, 4, 0, 1, 3, 5)
    site_rows = lattice_grid.reshape(tokens_dev, patch_len)
    frozen = site_parity(P_SIZE)[None, :] == parity.reshape(tokens_dev)[:, None]
    frozen_in = jnp.where(frozen, site_rows, 0.0).astype(jnp.bfloat16)
    embedded, normed = embed_rows(frozen_in, w_embed, b_embed, gain_in)
    blocks_dev = tokens_dev // BLK
    block_rows = lax.dynamic_slice_in_dim(
        block_list, lax.axis_index("tm") * blocks_dev, blocks_dev, 0
    )
    start_state = (
        jnp.full((HEADS, tokens_dev), floor_score, jnp.float32),
        jnp.zeros((HEADS, tokens_dev), jnp.float32),
        jnp.zeros((HEADS, tokens_dev, HS), jnp.float32),
    )
    qkv_rows = jnp.dot(normed, w_qkv, preferred_element_type=jnp.float32).astype(jnp.bfloat16)
    queries = qkv_rows[:, :D]

    def from_pair(block_parts):
        return (block_parts[0], block_parts[1])

    result = fold_rows(
        start_state,
        (
            lax.all_gather(qkv_rows[:, D : 2 * D], "tm", axis=0, tiled=True),
            lax.all_gather(qkv_rows[:, 2 * D :], "tm", axis=0, tiled=True),
        ),
        from_pair,
        queries,
        block_rows,
    )
    _, running_sum, running_out = result
    mixed = (running_out / running_sum[:, :, None]).transpose(1, 0, 2).reshape(tokens_dev, D)
    hidden = embedded + mixed
    normed_out = layer_norm(hidden, gain_out).astype(jnp.bfloat16)
    affine = jnp.dot(normed_out, w_head, preferred_element_type=jnp.float32) + b_head
    scale_log = jnp.tanh(affine[:, :patch_len])
    shift_val = affine[:, patch_len:]
    moved = jnp.where(frozen, site_rows, site_rows * jnp.exp(scale_log) + shift_val)
    log_det = jnp.sum(jnp.where(frozen, 0.0, scale_log))
    new_field = (
        moved.reshape(LY // P_SIZE, LZ // P_SIZE, P_SIZE, P_SIZE, P_SIZE, P_SIZE)
        .transpose(2, 3, 0, 4, 1, 5)
        .reshape(P_SIZE, P_SIZE, LY * LZ)
    )
    ahead_time = shifted(new_field[0:1].astype(jnp.bfloat16), "tm", -1).astype(jnp.float32)
    ahead_slab = shifted(new_field[:, 0:1].astype(jnp.bfloat16), "space", -1).astype(jnp.float32)
    next_time_field = jnp.concatenate([new_field[1:], ahead_time], axis=0)
    next_slab_field = jnp.concatenate([new_field[:, 1:], ahead_slab], axis=1)
    cube = new_field.reshape(P_SIZE, P_SIZE, LY, LZ)
    next_y_field = jnp.roll(cube, -1, 2).reshape(P_SIZE, P_SIZE, LY * LZ)
    next_z_field = jnp.roll(cube, -1, 3).reshape(P_SIZE, P_SIZE, LY * LZ)
    neighbours = next_time_field + next_slab_field
    neighbours = neighbours + next_y_field
    neighbours = neighbours + next_z_field
    squared = new_field * new_field
    density = (
        -2.0 * hopping * new_field * neighbours
        + squared
        + quartic * (squared - 1.0) * (squared - 1.0)
    )
    time_link = new_field * next_time_field
    slab_link = new_field * next_slab_field
    local_log = -0.5 * jnp.sum(lattice_field * lattice_field) - log_det
    local_act = jnp.sum(density)
    sum_log, sum_act = lax.psum((local_log, local_act), ("space", "tm"))
    site_count = lattice_field.size * lax.axis_size("space") * lax.axis_size("tm")
    totals = jnp.stack([sum_log / site_count - 0.5 * log_two_pi, sum_act / site_count]).astype(
        jnp.float32
    )
    return (new_field, density, time_link, slab_link, totals)


def solution(mesh):
    in_specs = (
        P("tm", "space", None),
        P("tm", "space", None),
        P(),
        P(),
        P(),
        P(),
        P(),
        P(),
        P(),
        P(),
    )
    out_specs = (
        P("tm", "space", None),
        P("tm", "space", None),
        P("tm", "space", None),
        P("tm", "space", None),
        P(),
    )
    return jax.shard_map(shards, mesh=mesh, in_specs=in_specs, out_specs=out_specs, check_vma=False)
```

profile of v0, /device:TPU:1, one launch (start us, length us, event | category | flops | bytes accessed | tf_op | source)
XLA Modules:
  0.0 584.1 jit_solution(14701347401462404792)
XLA Ops:
  7.3 6.7 %reshape.277 = f32[4,4,8,4,16,4]{5,4,3,2,1,0:T(8,128)} reshape(f32[4,4,2048]{2,1,0:T(4,128)} %param.14) | data formatting | bytes 262144 | tf_op jit(solution)/shard_map/reshape | solution.py:110
  14.0 5.7 copy.50
  32.6 102.8 %all-gather.3.cloned.1.call-done = bf16[2048,768]{1,0:T(8,128)(2,1)} async-done(((bf16[128,768]{1,0:T(8,128)(2,1)}), bf16[2048,768]{1,0:T(8,128)(2,1)}) %all-gather.3.cloned.1.call-update) | async-done | bytes 3145744 | tf_op jit(solution)/shard_map/all_gather | solution.py:135
  135.4 4.6 copy.53
  140.0 101.0 %all-gather.5.cloned.1.call-done = bf16[2048,768]{1,0:T(8,128)(2,1)} async-done(((bf16[128,768]{1,0:T(8,128)(2,1)}), bf16[2048,768]{1,0:T(8,128)(2,1)}) %all-gather.5.cloned.1.call-update) | async-done | bytes 3145744 | tf_op jit(solution)/shard_map/all_gather | solution.py:136
  241.0 4.7 copy.55
  247.1 100.4 %while.16 = (s32[]{:T(128)}, f32[12,128]{1,0:T(8,128)S(1)}, f32[12,128]{1,0:T(8,128)S(1)}, f32[12,128,64]{1,2,0:T(8,128)}, s32[16]{0:T(128)}, /*index=5*/s32[1,8...) while((s32[]{:T(128)}, f32[12,128]{1,0:T(8,128)S(1)}, ...), condition=%wide.region_9.10_spmd, body=%wide.region_2.9_spmd.sunk | while | flops 52304800 | bytes 7768141 | solution.py:99
  251.1 4.5 conditional.2
  259.6 4.5 conditional.2
  268.1 4.5 conditional.2
  280.6 4.5 conditional.2
  293.2 4.5 conditional.2
  301.7 4.5 conditional.2
  314.2 4.5 conditional.2
  338.9 4.5 conditional.2
  360.2 5.4 copy.60
  365.7 5.6 reshape.283
  371.3 4.3 reshape_reshape.3
  383.6 9.5 %collective-permute-start.1 = (bf16[4,1,2048]{2,1,0:T(2,128)(2,1)}, bf16[4,1,2048]{2,1,0:T(2,128)(2,1)}, u32[]{:S(2)}, u32[]{:S(2)}) collective-permute-start(bf16[4,1,2048]{2,1,0:T(2,128)(2,1)} %slice.87), channel_id=1, source_target_pairs={{0,496},{16,0},{32,16},{48,32},{64,48},{80,64},{96,80},{112,96},{1... | collective-permute-start | bytes 49160 | tf_op jit(solution)/shard_map/ppermute | solution.py:23
  398.0 9.9 %collective-permute-start = (bf16[1,4,2048]{2,1,0:T(4,128)(2,1)}, bf16[1,4,2048]{2,1,0:T(4,128)(2,1)S(1)}, u32[]{:S(2)}, u32[]{:S(2)}) collective-permute-start(bf16[1,4,2048]{2,1,0:T(4,128)(2,1)} %convert_element_type.46), channel_id=1, source_target_pairs={{0,15},{1,0},{2,1},{3,2},{4,3},{5,4},{6,5},{7,6},{8,7},{9,8},{10,9... | collective-permute-start | bytes 49160 | tf_op jit(solution)/shard_map/ppermute | solution.py:23
  416.9 4.4 reshape.287
  423.1 4.5 reshape.286
  427.6 4.6 copy.61
  432.2 5.7 copy.69
  437.8 5.6 copy.68
  443.5 5.1 reshape.288
  448.6 4.6 copy.66
  455.9 2.8 copy.64
  460.2 2.8 concatenate.33
  465.8 3.7 fusion.5
  469.5 4.6 slice.55
  474.1 98.3 %all-reduce = (f32[]{:T(128)}, f32[]{:T(128)}) all-reduce(f32[]{:T(128)} %fusion.5, f32[]{:T(128)S(6)} %sub.78), channel_id=1, replica_groups=mesh['space'=32,'tm'=16] {'space','tm'}, use_global_device_ids=true, to_apply=%region_16.17 | all-reduce | flops 2 | bytes 16 | tf_op jit(solution)/shard_map/psum | solution.py:176
  (217 shorter events, 137.6 us)
Async XLA Ops:
  7.2 18.5 %copy-start = (bf16[768,2304]{1,0:T(8,128)(2,1)S(1)}, bf16[768,2304]{1,0:T(8,128)(2,1)}, u32[]{:S(2)}) copy-start(bf16[768,2304]{1,0:T(8,128)(2,1)} %param.20) | copy-start | bytes 10616836
  7.2 128.2 %all-gather.3.cloned.1.call-start = ((), (), s32[]{:S(2)}) async-start(), calls=%async_computation | async-start | bytes 3342336 | tf_op jit(solution)/shard_map/all_gather | solution.py:135
  7.2 16.2 %copy-start.6 = (s32[256]{0:T(256)}, s32[256]{0:T(256)S(1)}, u32[]{:S(2)}) copy-start(s32[256]{0:T(256)S(1)} %and_select_fusion.1) | copy-start | bytes 3076
  14.0 9.5 %copy-start.4 = (f32[768]{0:T(1024)S(1)}, f32[768]{0:T(1024)}, u32[]{:S(2)}) copy-start(f32[768]{0:T(1024)} %param.18) | copy-start | bytes 9220
  14.0 9.5 %copy-start.10 = (s32[1,1,128]{2,1,0:T(1,128)S(1)}, s32[1,1,128]{2,1,0:T(1,128)}, u32[]{:S(2)}) copy-start(s32[1,1,128]{2,1,0:T(1,128)} %param.15) | copy-start | bytes 1540
  14.0 11.7 %copy-start.9 = (f32[768]{0:T(1024)S(1)}, f32[768]{0:T(1024)}, u32[]{:S(2)}) copy-start(f32[768]{0:T(1024)} %param.19) | copy-start | bytes 9220
  24.9 0.7 copy-start.3
  25.1 2.9 copy-start.8
  27.2 213.8 %all-gather.5.cloned.1.call-start = ((), (), s32[]{:S(2)}) async-start(), calls=%async_computation.1 | async-start | bytes 3342336 | tf_op jit(solution)/shard_map/all_gather | solution.py:136
  251.1 3.3 copy-start.1
  254.8 0.8 copy-start.2
  259.6 3.3 copy-start.1
  263.3 0.8 copy-start.2
  268.1 3.3 copy-start.1
  271.8 0.8 copy-start.2
  280.6 3.4 copy-start.1
  284.3 0.8 copy-start.2
  293.2 3.4 copy-start.1
  296.9 0.8 copy-start.2
  301.7 3.3 copy-start.1
  305.4 0.8 copy-start.2
  314.2 3.4 copy-start.1
  317.9 0.8 copy-start.2
  339.0 3.3 copy-start.1
  342.7 0.8 copy-start.2
  347.5 5.2 copy-start.5
  347.5 6.6 %copy-start.7 = (s32[256]{0:T(256)S(1)}, s32[256]{0:T(256)}, u32[]{:S(2)}) copy-start(s32[256]{0:T(256)} %copy-done.6) | copy-start | bytes 3076
  349.3 4.9 copy-start.11
  383.6 75.1 %collective-permute-start.1 = (bf16[4,1,2048]{2,1,0:T(2,128)(2,1)}, bf16[4,1,2048]{2,1,0:T(2,128)(2,1)}, u32[]{:S(2)}, u32[]{:S(2)}) collective-permute-start(bf16[4,1,2048]{2,1,0:T(2,128)(2,1)} %slice.87), channel_id=1, source_target_pairs={{0,496},{16,0},{32,16},{48,32},{64,48},{80,64},{96,80},{112,96},{1... | collective-permute-start | bytes 49160 | tf_op jit(solution)/shard_map/ppermute | solution.py:23
  398.0 55.8 %collective-permute-start = (bf16[1,4,2048]{2,1,0:T(4,128)(2,1)}, bf16[1,4,2048]{2,1,0:T(4,128)(2,1)S(1)}, u32[]{:S(2)}, u32[]{:S(2)}) collective-permute-start(bf16[1,4,2048]{2,1,0:T(4,128)(2,1)} %convert_element_type.46), channel_id=1, source_target_pairs={{0,15},{1,0},{2,1},{3,2},{4,3},{5,4},{6,5},{7,6},{8,7},{9,8},{10,9... | collective-permute-start | bytes 49160 | tf_op jit(solution)/shard_map/ppermute | solution.py:23
Sparse Core Ops, SparseCore 0:
  27.3 107.9 all-gather.2
  137.5 103.5 all-gather.4
where the time goes:
time: 587 us; the launch traced here: 584 us
  waiting for transfers between devices  205 us (35%)
  local copies, waits for them, and re-layouts  157 us (27%)
  blocking collectives  98.3 us (17%)
  other arithmetic  49 us (8%)
  loops' own time  22.7 us (4%)
  starting transfers between devices  19.5 us (3%)
  between operations  16.9 us (3%)
  matrix products  16.2 us (3%)
    all_gather x1, waiting for transfers between devices, shards(): lax.all_gather(qkv_rows[:, D:2 * D], 'tm', axis=0, tiled=True)  103 us
    all_gather x1, waiting for transfers between devices, shards(): lax.all_gather(qkv_rows[:, 2 * D:], 'tm', axis=0, tiled=True)  101 us
    psum x1, blocking collectives, shards(): sum_log, sum_act = lax.psum((local_log, local_act), ('space', 'tm'))  98.3 us
    dynamic_slice x24, local copies, waits for them, and re-layouts, fold_rows(): lax.scan(visit_block, carry_in, (jnp.arange(row_total // BLK, dtype=jnp.i...  29.4 us
    another operation x1, loops' own time, fold_rows(): lax.scan(visit_block, carry_in, (jnp.arange(row_total // BLK, dtype=jnp.i...  21.8 us
    reduce_or x16, other arithmetic, visit_block(): needed = jnp.any(block_rows == block_id)  21.6 us
    ppermute x2, starting transfers between devices, shifted(): lax.ppermute(x, axis, [(i, (i + by) % length) for i in range(length)])  19.4 us
    concatenate x4, local copies, waits for them, and re-layouts, shards(): next_slab_field = jnp.concatenate([new_field[:, 1:], ahead_slab], axis=1)  15.3 us
  transfers between devices with their start and end apart: 4, of which 2 were waited for; matrix products, arithmetic and copies ran while one was open for 11% of the time, Pallas kernels for 0%

commit v1 on v0

--- a/solution.py
+++ b/solution.py
@@ -16,6 +16,11 @@
 epsilon = 1e-05
 log_two_pi = math.log(2.0 * math.pi)
 floor_score = -1e30
+
+
+def exchange_gather(array, mesh_axis, dim):
+    sent = jnp.stack([array] * lax.axis_size(mesh_axis))
+    return jnp.concatenate(lax.all_to_all(sent, mesh_axis, 0, 0), axis=dim)
 
 
 def shifted(x, axis, by):
@@ -133,7 +138,7 @@
         start_state,
         (
             lax.all_gather(qkv_rows[:, D : 2 * D], "tm", axis=0, tiled=True),
-            lax.all_gather(qkv_rows[:, 2 * D :], "tm", axis=0, tiled=True),
+            exchange_gather(qkv_rows[:, 2 * D :], "tm", 0),
         ),
         from_pair,
         queries,

time: 587 us -> 565 us (0.963)
  waiting for transfers between devices: 205 us -> 166 us
  starting transfers between devices: 19.5 us -> 29 us
  blocking collectives: 98.3 us -> 105 us
    all_gather x1 -> x0, waiting for transfers between devices: 101 us -> none  [shards(): lax.all_gather(qkv_rows[:, 2 * D:], 'tm', axis=0, tiled=True)]
    all_gather x1, waiting for transfers between devices: 103 us -> 165 us  [shards(): lax.all_gather(qkv_rows[:, D:2 * D], 'tm', axis=0, tiled=True)]
    all_to_all x0 -> x1, starting transfers between devices: none -> 14.2 us  [exchange_gather(): return jnp.concatenate(lax.all_to_all(sent, mesh_axis, 0, 0), axis=dim)]
    psum x1, blocking collectives: 98.3 us -> 105 us  [shards(): sum_log, sum_act = lax.psum((local_log, local_act), ('space', 'tm'))]
  transfers between devices with their start and end apart: 4 -> 4, of which waited for: 2 -> 1; matrix products, arithmetic and copies ran while one was open for 11% -> 11% of each run, Pallas kernels for 0% -> 0%
where the time goes in v1:
time: 565 us; the launch traced here: 562 us
  waiting for transfers between devices  166 us (29%)
  local copies, waits for them, and re-layouts  157 us (28%)
  blocking collectives  105 us (19%)
  other arithmetic  49 us (9%)
  starting transfers between devices  29 us (5%)
  loops' own time  22.6 us (4%)
  between operations  16.8 us (3%)
  matrix products  16.2 us (3%)
    all_gather x1, waiting for transfers between devices, shards(): lax.all_gather(qkv_rows[:, D:2 * D], 'tm', axis=0, tiled=True)  165 us
    psum x1, blocking collectives, shards(): sum_log, sum_act = lax.psum((local_log, local_act), ('space', 'tm'))  105 us
    dynamic_slice x24, local copies, waits for them, and re-layouts, fold_rows(): lax.scan(visit_block, carry_in, (jnp.arange(row_total // BLK, dtype=jnp.i...  29.4 us
    another operation x1, loops' own time, fold_rows(): lax.scan(visit_block, carry_in, (jnp.arange(row_total // BLK, dtype=jnp.i...  21.8 us
    reduce_or x16, other arithmetic, visit_block(): needed = jnp.any(block_rows == block_id)  21.6 us
    concatenate x4, local copies, waits for them, and re-layouts, shards(): next_slab_field = jnp.concatenate([new_field[:, 1:], ahead_slab], axis=1)  15.3 us
    ppermute x2, starting transfers between devices, shifted(): lax.ppermute(x, axis, [(i, (i + by) % length) for i in range(length)])  14.8 us
    all_to_all x1, starting transfers between devices, exchange_gather(): return jnp.concatenate(lax.all_to_all(sent, mesh_axis, 0, 0), axis=dim)  14.2 us
  transfers between devices with their start and end apart: 4, of which 1 were waited for; matrix products, arithmetic and copies ran while one was open for 11% of the time, Pallas kernels for 0%

profile of v1, /device:TPU:1, one launch (start us, length us, event | category | flops | bytes accessed | tf_op | source)
XLA Modules:
  0.0 562.1 jit_solution(16625260063676555853)
XLA Ops:
  7.2 6.7 %reshape.276 = f32[4,4,8,4,16,4]{5,4,3,2,1,0:T(8,128)} reshape(f32[4,4,2048]{2,1,0:T(4,128)} %param.14) | data formatting | bytes 262144 | tf_op jit(solution)/shard_map/reshape | solution.py:115
  13.9 5.7 %copy.50 = f32[8,16,4,4,4,4]{1,0,5,4,3,2:T(8,128)} copy(f32[8,16,4,4,4,4]{5,1,4,0,3,2:T(8,128)} %bitcast.52) | data formatting | bytes 262144 | tf_op jit(solution)/shard_map/transpose | solution.py:117
  28.9 3.2 stack.8
  32.2 14.2 %all-to-all-start = ((bf16[16,128,768]{1,2,0:T(8,128)(2,1)}), bf16[16,128,768]{1,2,0:T(8,128)(2,1)}, u32[]{:S(2)}, u32[]{:S(2)}) async-start(bf16[16,128,768]{1,2,0:T(8,128)(2,1)} %stack.8), calls=%async_computation | async-start | bytes 6291456 | tf_op jit(solution)/shard_map/all_to_all | solution.py:23
  51.7 165.4 %all-gather.2.cloned.1.call-done = bf16[2048,768]{1,0:T(8,128)(2,1)} async-done(((bf16[128,768]{1,0:T(8,128)(2,1)}), bf16[2048,768]{1,0:T(8,128)(2,1)}) %all-gather.2.cloned.1.call-update) | async-done | bytes 3145744 | tf_op jit(solution)/shard_map/all_gather | solution.py:140
  217.2 4.7 copy.54
  223.2 100.4 %while.16 = (s32[]{:T(128)}, f32[12,128]{1,0:T(8,128)S(1)}, f32[12,128]{1,0:T(8,128)S(1)}, f32[12,128,64]{1,2,0:T(8,128)}, s32[16]{0:T(128)}, /*index=5*/s32[1,8...) while((s32[]{:T(128)}, f32[12,128]{1,0:T(8,128)S(1)}, ...), condition=%wide.region_9.10_spmd, body=%wide.region_2.9_spmd.sunk | while | flops 52304800 | bytes 7768141 | solution.py:104
  227.2 4.5 conditional.2
  235.7 4.5 conditional.2
  244.2 4.5 conditional.2
  256.7 4.5 conditional.2
  269.3 4.5 conditional.2
  277.8 4.5 conditional.2
  290.3 4.5 conditional.2
  315.1 4.5 conditional.2
  336.3 5.4 copy.60
  341.8 5.6 reshape.281
  347.4 4.3 reshape_reshape.3
  359.7 12.7 %collective-permute-start.1 = (bf16[4,1,2048]{2,1,0:T(2,128)(2,1)}, bf16[4,1,2048]{2,1,0:T(2,128)(2,1)}, u32[]{:S(2)}, u32[]{:S(2)}) collective-permute-start(bf16[4,1,2048]{2,1,0:T(2,128)(2,1)} %slice.87), channel_id=1, source_target_pairs={{0,496},{16,0},{32,16},{48,32},{64,48},{80,64},{96,80},{112,96},{1... | collective-permute-start | bytes 49160 | tf_op jit(solution)/shard_map/ppermute | solution.py:28
  388.4 4.4 reshape.285
  394.6 4.5 reshape.284
  399.1 4.6 copy.61
  403.7 5.7 %copy.69 = f32[4,4,8,4,16,4]{4,2,5,3,1,0:T(8,128)} copy(f32[4,4,8,4,16,4]{5,4,3,2,1,0:T(8,128)} %reshape.285) | data formatting | bytes 262144 | tf_op jit(solution)/shard_map/reshape | solution.py:167
  409.4 5.6 %copy.68 = f32[4,4,8,4,16,4]{4,2,5,3,1,0:T(8,128)} copy(f32[4,4,8,4,16,4]{5,4,3,2,1,0:T(8,128)} %reshape.284) | data formatting | bytes 262144 | tf_op jit(solution)/shard_map/reshape | solution.py:166
  415.0 5.1 reshape.286
  420.1 4.6 copy.66
  427.5 2.8 copy.64
  431.7 2.8 concatenate.33
  434.5 2.8 copy.67
  437.3 3.7 fusion.5
  441.1 4.6 slice.55
  445.7 104.9 %all-reduce = (f32[]{:T(128)}, f32[]{:T(128)}) all-reduce(f32[]{:T(128)} %fusion.5, f32[]{:T(128)S(6)} %sub.78), channel_id=1, replica_groups=mesh['space'=32,'tm'=16] {'space','tm'}, use_global_device_ids=true, to_apply=%region_16.17 | all-reduce | flops 2 | bytes 16 | tf_op jit(solution)/shard_map/psum | solution.py:181
  (217 shorter events, 138.7 us)
Async XLA Ops:
  7.2 18.5 %copy-start = (bf16[768,2304]{1,0:T(8,128)(2,1)S(1)}, bf16[768,2304]{1,0:T(8,128)(2,1)}, u32[]{:S(2)}) copy-start(bf16[768,2304]{1,0:T(8,128)(2,1)} %param.20) | copy-start | bytes 10616836
  7.2 16.2 %copy-start.6 = (s32[256]{0:T(256)}, s32[256]{0:T(256)S(1)}, u32[]{:S(2)}) copy-start(s32[256]{0:T(256)S(1)} %and_select_fusion.1) | copy-start | bytes 3076
  13.9 9.5 %copy-start.4 = (f32[768]{0:T(1024)S(1)}, f32[768]{0:T(1024)}, u32[]{:S(2)}) copy-start(f32[768]{0:T(1024)} %param.18) | copy-start | bytes 9220
  13.9 9.5 %copy-start.10 = (s32[1,1,128]{2,1,0:T(1,128)S(1)}, s32[1,1,128]{2,1,0:T(1,128)}, u32[]{:S(2)}) copy-start(s32[1,1,128]{2,1,0:T(1,128)} %param.15) | copy-start | bytes 1540
  13.9 11.7 %copy-start.9 = (f32[768]{0:T(1024)S(1)}, f32[768]{0:T(1024)}, u32[]{:S(2)}) copy-start(f32[768]{0:T(1024)} %param.19) | copy-start | bytes 9220
  24.9 0.8 copy-start.3
  32.1 14.9 %copy-start.8 = (s32[16,8]{0,1:T(8,128)S(1)}, s32[16,8]{0,1:T(8,128)}, u32[]{:S(2)}) copy-start(s32[16,8]{0,1:T(8,128)} %param.16) | copy-start | bytes 1540
  32.2 189.7 %all-to-all-start = ((bf16[16,128,768]{1,2,0:T(8,128)(2,1)}), bf16[16,128,768]{1,2,0:T(8,128)(2,1)}, u32[]{:S(2)}, u32[]{:S(2)}) async-start(bf16[16,128,768]{1,2,0:T(8,128)(2,1)} %stack.8), calls=%async_computation | async-start | bytes 6291456 | tf_op jit(solution)/shard_map/all_to_all | solution.py:23
  46.3 170.8 %all-gather.2.cloned.1.call-start = ((), (), s32[]{:S(2)}) async-start(), calls=%async_computation.1 | async-start | bytes 3342336 | tf_op jit(solution)/shard_map/all_gather | solution.py:140
  227.2 3.3 copy-start.1
  230.9 0.8 copy-start.2
  235.7 3.3 copy-start.1
  239.4 0.8 copy-start.2
  244.2 3.3 copy-start.1
  247.9 0.8 copy-start.2
  256.7 3.4 copy-start.1
  260.4 0.8 copy-start.2
  269.3 3.4 copy-start.1
  273.0 0.8 copy-start.2
  277.8 3.3 copy-start.1
  281.5 0.8 copy-start.2
  290.4 3.4 copy-start.1
  294.1 0.8 copy-start.2
  315.1 3.3 copy-start.1
  318.8 0.8 copy-start.2
  323.6 5.2 copy-start.5
  323.6 6.6 %copy-start.7 = (s32[256]{0:T(256)S(1)}, s32[256]{0:T(256)}, u32[]{:S(2)}) copy-start(s32[256]{0:T(256)} %copy-done.6) | copy-start | bytes 3076
  325.4 4.9 copy-start.11
  359.7 70.5 %collective-permute-start.1 = (bf16[4,1,2048]{2,1,0:T(2,128)(2,1)}, bf16[4,1,2048]{2,1,0:T(2,128)(2,1)}, u32[]{:S(2)}, u32[]{:S(2)}) collective-permute-start(bf16[4,1,2048]{2,1,0:T(2,128)(2,1)} %slice.87), channel_id=1, source_target_pairs={{0,496},{16,0},{32,16},{48,32},{64,48},{80,64},{96,80},{112,96},{1... | collective-permute-start | bytes 49160 | tf_op jit(solution)/shard_map/ppermute | solution.py:28
  377.4 48.0 %collective-permute-start = (bf16[1,4,2048]{2,1,0:T(4,128)(2,1)}, bf16[1,4,2048]{2,1,0:T(4,128)(2,1)S(1)}, u32[]{:S(2)}, u32[]{:S(2)}) collective-permute-start(bf16[1,4,2048]{2,1,0:T(4,128)(2,1)} %convert_element_type.46), channel_id=1, source_target_pairs={{0,15},{1,0},{2,1},{3,2},{4,3},{5,4},{6,5},{7,6},{8,7},{9,8},{10,9... | collective-permute-start | bytes 49160 | tf_op jit(solution)/shard_map/ppermute | solution.py:28
Sparse Core Ops, SparseCore 0:
  49.2 167.8 all-gather.1
